TPU v7x, 128 devices: a whole 4x4x4 slice. The times are simulated.
128 devices in a mesh: req: 16 (over x, y), vocab: 8 (over z, core).
Axes of the slice: x: 4, y: 4, z: 4, core: 2. Of those that a mesh axis runs over, the one named last changes fastest.
Arguments:
- hidden: bfloat16 [64, 128, 2048], P('req'), may hold values from -1000 to 1000
- gain: float32 [2048], replicated, may hold values from 0.5 to 1.5
- embedding: bfloat16 [76800, 2048], P('vocab', 'req'), may hold values from -16 to 16
- targets: int32 [64, 128], P('req'), may hold values from 0 to 76799
- span_start: int32 [64], P('req'), may hold values from 0 to 127, as said below
- span_len: int32 [64], P('req'), may hold values from 1 to 128
- deal_order: int32 [64], replicated, may hold values from 0 to 63, as said below
Outputs:
- logprob: float32 [64, 128], P('req')
- entropy: float32 [64, 128], P('req')
Inputs may be any that keep to these rules, and one draw needn't show every extreme that they name: deal_order is a permutation of the requests; the span lengths of the 4 requests dealt to one group add up to at most 224, exactly 224 for some group. span_start + span_len <= 128 for every request.
All inputs are finite; a program needn't handle non-finite values.
Results may differ from a plain program's by a relative error of at most 0.0029.
Values may be sent and summed in bfloat16 or wider, within the bound.
No kernel may reach another device: no remote copies, remote signals or barrier semaphores. Data moves between devices by JAX's collectives and lax.ppermute only.
A program may use at most 128 MiB of HBM per device.

v0:
```python
import jax
import jax.numpy as jnp
from jax import lax
from jax.sharding import PartitionSpec as P

CAP = 224
eps = 1e-06


def compact_plan(row_base, lengths, capacity):
    offsets = jnp.cumsum(lengths) - lengths
    counter = jnp.arange(capacity, dtype=jnp.int32)
    member = jnp.sum((counter[:, None] >= offsets[None, :]).astype(jnp.int32), axis=1) - 1
    member_hot = (member[:, None] == jnp.arange(lengths.shape[0], dtype=jnp.int32)[None, :]).astype(
        jnp.int32
    )
    row_index = jnp.sum(member_hot * (row_base - offsets)[None, :], axis=1) + counter
    in_span = counter < jnp.sum(lengths)
    return (row_index, in_span)


def normalize(rows, gain):
    wide_rows = rows.astype(jnp.float32)
    scale = lax.rsqrt(jnp.mean(wide_rows * wide_rows, axis=1, keepdims=True) + eps)
    return (wide_rows * scale * gain).astype(jnp.bfloat16)


def shards(hidden, gain, embedding, targets, span_start, span_len, deal_order):
    per_dev = hidden.shape[0]
    slot_len = hidden.shape[1]
    width = hidden.shape[2]
    total = deal_order.shape[0]
    voc_local = embedding.shape[0]
    here = lax.axis_index("req")
    positions = jnp.arange(total, dtype=jnp.int32)
    source_of = jnp.sum(
        jnp.where(deal_order[None, :] == positions[:, None], positions[None, :], 0), axis=1
    )
    all_starts, all_lengths = (
        lax.all_gather(span_start, "req", axis=0, tiled=True),
        lax.all_gather(span_len, "req", axis=0, tiled=True),
    )
    my_slots = here * per_dev + jnp.arange(per_dev, dtype=jnp.int32)
    members = jnp.sum(
        jnp.where(my_slots[:, None] == positions[None, :], source_of[None, :], 0), axis=1
    )
    member_hot = members[:, None] == positions[None, :]
    lengths = jnp.sum(jnp.where(member_hot, all_lengths[None, :], 0), axis=1)
    starts = jnp.sum(jnp.where(member_hot, all_starts[None, :], 0), axis=1)
    row_base = jnp.arange(per_dev, dtype=jnp.int32) * slot_len + starts
    row_index, in_span = compact_plan(row_base, lengths, CAP)
    safe_index = jnp.where(in_span, row_index, 0)
    spread_rows, spread_marks = (
        lax.all_to_all(hidden, "req", split_axis=1, concat_axis=0, tiled=True),
        lax.all_to_all(targets, "req", split_axis=1, concat_axis=0, tiled=True),
    )
    dealt_rows = jnp.take(spread_rows, source_of, axis=0)
    dealt_marks = jnp.take(spread_marks, source_of, axis=0)
    home_rows, home_marks = (
        lax.all_to_all(dealt_rows, "req", split_axis=0, concat_axis=1, tiled=True),
        lax.all_to_all(dealt_marks, "req", split_axis=0, concat_axis=1, tiled=True),
    )
    rows = jnp.take(home_rows.reshape(per_dev * slot_len, width), safe_index, axis=0)
    target_ids = jnp.where(
        in_span, jnp.take(home_marks.reshape(per_dev * slot_len), safe_index), -1
    )
    normed = normalize(rows, gain)
    logits = lax.dot_general(
        normed,
        lax.all_gather(embedding, "req", axis=1, tiled=True),
        (((1,), (1,)), ((), ())),
        preferred_element_type=jnp.float32,
    )
    local_top = jnp.max(logits, axis=1)
    shifted = logits - local_top[:, None]
    weights = jnp.exp(shifted)
    local_mass = jnp.sum(weights, axis=1)
    local_spread = jnp.sum(weights * shifted, axis=1)
    local_ids = target_ids - lax.axis_index("vocab") * voc_local
    local_target = jnp.sum(
        jnp.where(
            jnp.arange(voc_local, dtype=jnp.int32)[None, :] == local_ids[:, None], logits, 0.0
        ),
        axis=1,
    )
    row_top = lax.pmax(local_top, "vocab")
    factor = jnp.exp(local_top - row_top)
    row_mass, row_spread, row_target = lax.psum(
        (
            factor * local_mass,
            factor * (local_spread + (local_top - row_top) * local_mass),
            local_target,
        ),
        "vocab",
    )
    log_mass = jnp.log(row_mass)
    compact_logprob = jnp.where(in_span, row_target - row_top - log_mass, 0.0)
    compact_entropy = jnp.where(in_span, log_mass - row_spread / row_mass, 0.0)
    spot = jnp.where(in_span, row_index, per_dev * slot_len)
    dealt_logprob = (
        jnp.zeros((per_dev * slot_len,), jnp.float32)
        .at[spot]
        .set(compact_logprob, mode="drop")
        .reshape(per_dev, slot_len)
    )
    dealt_entropy = (
        jnp.zeros((per_dev * slot_len,), jnp.float32)
        .at[spot]
        .set(compact_entropy, mode="drop")
        .reshape(per_dev, slot_len)
    )
    wide_logprob, wide_entropy = (
        lax.all_to_all(dealt_logprob, "req", split_axis=1, concat_axis=0, tiled=True),
        lax.all_to_all(dealt_entropy, "req", split_axis=1, concat_axis=0, tiled=True),
    )
    home_logprob = jnp.take(wide_logprob, deal_order, axis=0)
    home_entropy = jnp.take(wide_entropy, deal_order, axis=0)
    out_logprob, out_entropy = (
        lax.all_to_all(home_logprob, "req", split_axis=0, concat_axis=1, tiled=True),
        lax.all_to_all(home_entropy, "req", split_axis=0, concat_axis=1, tiled=True),
    )
    return (out_logprob, out_entropy)


def solution(mesh):
    in_specs = (
        P("req", None, None),
        P(),
        P("vocab", "req"),
        P("req", None),
        P("req"),
        P("req"),
        P(),
    )
    out_specs = (P("req", None), P("req", None))
    return jax.shard_map(shards, mesh=mesh, in_specs=in_specs, out_specs=out_specs, check_vma=False)
```

profile of v0, /device:TPU:0, one launch (start us, length us, event | category | flops | bytes accessed | tf_op | source)
XLA Modules:
  0.0 401.7 jit_solution(16751751695467223779)
XLA Ops:
  7.2 0.0 all-gather.2.cloned.1.call-start
  7.2 0.7 all-gather.2.cloned.1.call-update
  7.9 0.1 all_to_all.104
  8.0 0.6 copy.39
  8.6 7.1 %all-to-all-start = ((s32[4,16,8]{2,0,1:T(4,128)}), s32[4,16,8]{2,0,1:T(4,128)S(1)}, u32[]{:S(2)}, u32[]{:S(2)}) async-start(s32[4,16,8]{2,0,1:T(4,128)} %copy.39), calls=%async_computation | async-start | bytes 65536 | tf_op jit(solution)/shard_map/all_to_all | solution.py:55
  15.8 2.9 copy.41
  18.7 4.7 %all-to-all-done = s32[4,16,8]{2,0,1:T(4,128)S(1)} async-done(((s32[4,16,8]{2,0,1:T(4,128)}), s32[4,16,8]{2,0,1:T(4,128)S(1)}, u32[]{:S(2)}, u32[]{:S(2)}) %all-to-all-start) | async-done | bytes 2080 | tf_op jit(solution)/shard_map/all_to_all | solution.py:55
  23.4 3.7 all-to-all-start.2
  27.2 0.1 select_reduce_fusion.1
  27.3 0.1 reduce_sum.113
  27.4 0.6 gather_fusion
  28.0 0.7 broadcast_select_fusion.5
  28.7 39.2 %all-to-all-done.2 = bf16[4,128,2048]{2,0,1:T(4,128)(2,1)S(1)} async-done(((bf16[4,128,2048]{2,0,1:T(4,128)(2,1)}), bf16[4,128,2048]{2,0,1:T(4,128)(2,1)S(1)}, u32[]{:S(2)}, u32[]{:S(2)}) %all-to-all-start.2) | async-done | bytes 2097184 | tf_op jit(solution)/shard_map/all_to_all | solution.py:54
  67.9 4.7 %all-to-all-start.1 = ((s32[16,4,8]{2,1,0:T(4,128)}), s32[16,4,8]{2,1,0:T(4,128)S(1)}, u32[]{:S(2)}, u32[]{:S(2)}) async-start(s32[16,4,8]{2,1,0:T(4,128)} %broadcast_select_fusion.5), calls=%async_computation.1 | async-start | bytes 65536 | tf_op jit(solution)/shard_map/all_to_all | solution.py:61
  72.6 1.2 copy.50
  73.8 1.4 copy.43
  75.2 2.3 gather_fusion.2
  77.5 1.6 broadcast_select_fusion
  79.1 1.3 all-to-all-done.1
  80.4 6.1 %all-to-all-start.3 = ((bf16[64,8,2048]{2,1,0:T(8,128)(2,1)}), bf16[64,8,2048]{2,1,0:T(8,128)(2,1)S(1)}, u32[]{:S(2)}, u32[]{:S(2)}) async-start(bf16[64,8,2048]{2,1,0:T(8,128)(2,1)} %broadcast_select_fusion), calls=%async_computation.3 | async-start | bytes 4194304 | tf_op jit(solution)/shard_map/all_to_all | solution.py:60
  86.5 0.6 dynamic-slice
  87.7 0.2 dynamic-update-slice
  88.0 0.2 dynamic-update-slice.1
  88.2 37.1 %all-reduce.2 = (s32[64]{0:T(128)S(1)}, s32[64]{0:T(128)S(1)}) all-reduce(s32[64]{0:T(128)S(1)} %dynamic-update-slice, s32[64]{0:T(128)S(1)} %dynamic-update-slice.1), channel_id=1, replica_groups=mesh['req'=16,'vocab'=8] {'req'}, use_global_device_ids=true, to_apply=%add | all-reduce | flops 128 | bytes 1024
  125.3 0.2 select_reduce_fusion.6
  125.5 0.7 select_reduce_fusion.4
  126.2 0.2 reduce-window.7
  126.4 0.1 convert_reduce_fusion
  126.5 0.1 select_reduce_fusion.2
  126.6 0.7 compare_select_fusion.1
  127.3 0.1 reshape.187
  127.4 1.9 gather_fusion.1
  129.3 0.7 select_subtract_fusion
  130.0 0.0 all-to-all-done.3
  130.0 1.3 copy-done
  131.3 1.8 copy.44
  133.1 0.0 copy-start.3
  133.1 1.3 gather_fusion.3
  134.4 0.4 fusion.1
  134.8 157.2 %all-gather.2.cloned.1.call-done = bf16[9600,2048]{1,0:T(8,128)(2,1)} async-done(((bf16[9600,128]{1,0:T(8,128)(2,1)}), bf16[9600,2048]{1,0:T(8,128)(2,1)}) %all-gather.2.cloned.1.call-update) | async-done | bytes 39321616 | tf_op jit(solution)/shard_map/all_gather | solution.py:70
  291.9 0.0 copy-done.3
  291.9 21.5 %fusion.14 = (f32[224]{0:T(256)S(1)}, f32[224,9600]{1,0:T(8,128)}) fusion(bf16[9600,2048]{1,0:T(8,128)(2,1)} %all-gather.2.cloned.1.call-done, f32[2048]{0:T(1024)S(1)} %copy-done.3, f32[224]{0:T(256)S(1)} %add_rsqrt_fusion, bf16[224,2048]{1,0:T(8,128)(2,1)S(1)} %gather_fusion.3, pred[224]{0:T(512)(128)(4,1)S(1)} %get-tuple-element.15), kind=kOutput, calls=%fused_computation.73 | convolution fusion | flops 8812482560 | bytes 48850912 | tf_op jit(solution)/shard_map/dot_general | solution.py:68
  313.5 13.6 %pmax.7 = f32[224]{0:T(256)S(1)} all-reduce(f32[224]{0:T(256)S(1)} %get-tuple-element.26), channel_id=1, replica_groups=mesh['req'=16,'vocab'=8] {'vocab'}, use_global_device_ids=true, to_apply=%region_12.13 | all-reduce | flops 224 | bytes 1792 | tf_op jit(solution)/shard_map/pmax | solution.py:86
  327.1 5.3 %fusion = (f32[224]{0:T(256)S(1)}, f32[224]{0:T(256)S(1)}, f32[224]{0:T(256)S(1)}) fusion(f32[224,9600]{1,0:T(8,128)} %get-tuple-element.27, f32[224]{0:T(256)S(1)} %get-tuple-element.26, s32[224]{0:T(256)S(1)} %get-tuple-element.14), kind=kLoop, calls=%fused_computation.10 | loop fusion | flops 15052128 | bytes 8606080 | tf_op jit(solution)/shard_map/reduce_sum | solution.py:78
  332.4 12.4 %all-reduce.3 = (f32[224]{0:T(256)S(1)}, f32[224]{0:T(256)S(1)}, f32[224]{0:T(256)S(1)}) all-reduce(f32[224]{0:T(256)S(1)} %get-tuple-element.5, f32[224]{0:T(256)S(1)} %get-tuple-element.19, f32[224]{0:T(256)S(1)} %get-tuple-element.18), channel_id=1, replica_groups=mesh['req'=16,'vocab'=8] {'vocab'}, use_global_device_ids=true, to_apply=%region_10.11 | all-reduce | flops 672 | bytes 5376 | tf_op jit(solution)/shard_map/psum | solution.py:88
  344.8 0.7 subtract_select_fusion
  345.5 1.3 scatter_custom_fusion.1
  346.8 0.1 all_to_all.125
  346.9 0.6 copy.47
  347.5 4.9 %all-to-all-start.6 = ((f32[4,16,8]{2,0,1:T(4,128)}), f32[4,16,8]{2,0,1:T(4,128)S(1)}, u32[]{:S(2)}, u32[]{:S(2)}) async-start(f32[4,16,8]{2,0,1:T(4,128)} %copy.47), calls=%async_computation.6 | async-start | bytes 65536 | tf_op jit(solution)/shard_map/all_to_all | solution.py:114
  352.4 1.3 scatter_custom_fusion
  353.7 0.1 all_to_all.117
  353.8 0.6 copy.45
  354.5 5.6 %all-to-all-done.6 = f32[4,16,8]{2,0,1:T(4,128)S(1)} async-done(((f32[4,16,8]{2,0,1:T(4,128)}), f32[4,16,8]{2,0,1:T(4,128)S(1)}, u32[]{:S(2)}, u32[]{:S(2)}) %all-to-all-start.6) | async-done | bytes 2080 | tf_op jit(solution)/shard_map/all_to_all | solution.py:114
  360.0 3.5 all-to-all-start.4
  363.5 0.6 gather_fusion.5
  364.1 6.9 %all-to-all-done.4 = f32[4,16,8]{2,0,1:T(4,128)S(1)} async-done(((f32[4,16,8]{2,0,1:T(4,128)}), f32[4,16,8]{2,0,1:T(4,128)S(1)}, u32[]{:S(2)}, u32[]{:S(2)}) %all-to-all-start.4) | async-done | bytes 2080 | tf_op jit(solution)/shard_map/all_to_all | solution.py:113
  371.1 0.6 gather_fusion.4
  371.7 0.7 broadcast_select_fusion.3
  372.4 10.7 %all_to_all.141 = f32[16,4,8]{2,1,0:T(4,128)S(1)} all-to-all(f32[16,4,8]{2,1,0:T(4,128)S(1)} %bitcast.49), channel_id=1, replica_groups=mesh['req'=16,'vocab'=8] {'req'}, dimensions={0} | all-to-all | bytes 4096 | tf_op jit(solution)/shard_map/all_to_all | solution.py:119
  383.1 3.5 all-to-all-start.7
  386.6 0.7 all_to_all.124
  387.3 6.9 %all-to-all-done.7 = f32[16,4,8]{2,1,0:T(4,128)S(1)} async-done(((f32[16,4,8]{2,1,0:T(4,128)}), f32[16,4,8]{2,1,0:T(4,128)S(1)}, u32[]{:S(2)}, u32[]{:S(2)}) %all-to-all-start.7) | async-done | bytes 2080 | tf_op jit(solution)/shard_map/all_to_all | solution.py:120
  394.2 0.7 all_to_all.132
  (31 shorter events, 0.1 us)
Async XLA Ops:
  7.2 0.8 copy-start.2
  7.2 8.6 %copy-start.1 = (bf16[4,128,2048]{2,1,0:T(8,128)(2,1)S(1)}, bf16[4,128,2048]{2,1,0:T(8,128)(2,1)}, u32[]{:S(2)}) copy-start(bf16[4,128,2048]{2,1,0:T(8,128)(2,1)} %param.9) | copy-start | bytes 6291460
  7.2 284.8 %all-gather.2.cloned.1.call-start = ((), (), s32[]{:S(2)}) async-start(), calls=%async_computation.8 | async-start | bytes 41779200 | tf_op jit(solution)/shard_map/all_gather | solution.py:70
  8.6 14.8 %all-to-all-start = ((s32[4,16,8]{2,0,1:T(4,128)}), s32[4,16,8]{2,0,1:T(4,128)S(1)}, u32[]{:S(2)}, u32[]{:S(2)}) async-start(s32[4,16,8]{2,0,1:T(4,128)} %copy.39), calls=%async_computation | async-start | bytes 65536 | tf_op jit(solution)/shard_map/all_to_all | solution.py:55
  18.7 8.4 %copy-start.6 = (s32[64]{0:T(128)S(1)}, s32[64]{0:T(128)}, u32[]{:S(2)}) copy-start(s32[64]{0:T(128)} %param.15) | copy-start | bytes 772
  23.4 44.5 %all-to-all-start.2 = ((bf16[4,128,2048]{2,0,1:T(4,128)(2,1)}), bf16[4,128,2048]{2,0,1:T(4,128)(2,1)S(1)}, u32[]{:S(2)}, u32[]{:S(2)}) async-start(bf16[4,128,2048]{2,0,1:T(4,128)(2,1)} %copy.41), calls=%async_computation.2 | async-start | bytes 4194304 | tf_op jit(solution)/shard_map/all_to_all | solution.py:54
  67.9 12.5 %all-to-all-start.1 = ((s32[16,4,8]{2,1,0:T(4,128)}), s32[16,4,8]{2,1,0:T(4,128)S(1)}, u32[]{:S(2)}, u32[]{:S(2)}) async-start(s32[16,4,8]{2,1,0:T(4,128)} %broadcast_select_fusion.5), calls=%async_computation.1 | async-start | bytes 65536 | tf_op jit(solution)/shard_map/all_to_all | solution.py:61
  79.1 7.4 %copy-start.7 = (u32[128]{0:T(128)S(1)}, u32[128]{0:T(128)}, u32[]{:S(2)}) copy-start(u32[128]{0:T(128)} %constant.108) | copy-start | bytes 1540
  79.1 8.7 %copy-start.4 = (s32[4]{0:T(128)S(1)}, s32[4]{0:T(128)}, u32[]{:S(2)}) copy-start(s32[4]{0:T(128)} %param.14) | copy-start | bytes 52
  79.1 8.9 %copy-start.5 = (s32[4]{0:T(128)S(1)}, s32[4]{0:T(128)}, u32[]{:S(2)}) copy-start(s32[4]{0:T(128)} %param.13) | copy-start | bytes 52
  80.4 49.6 %all-to-all-start.3 = ((bf16[64,8,2048]{2,1,0:T(8,128)(2,1)}), bf16[64,8,2048]{2,1,0:T(8,128)(2,1)S(1)}, u32[]{:S(2)}, u32[]{:S(2)}) async-start(bf16[64,8,2048]{2,1,0:T(8,128)(2,1)} %broadcast_select_fusion), calls=%async_computation.3 | async-start | bytes 4194304 | tf_op jit(solution)/shard_map/all_to_all | solution.py:60
  130.0 1.3 copy-start
  133.1 158.8 %copy-start.3 = (f32[2048]{0:T(1024)S(1)}, f32[2048]{0:T(1024)}, u32[]{:S(2)}) copy-start(f32[2048]{0:T(1024)} %param.10) | copy-start | bytes 24580
  347.5 12.6 %all-to-all-start.6 = ((f32[4,16,8]{2,0,1:T(4,128)}), f32[4,16,8]{2,0,1:T(4,128)S(1)}, u32[]{:S(2)}, u32[]{:S(2)}) async-start(f32[4,16,8]{2,0,1:T(4,128)} %copy.47), calls=%async_computation.6 | async-start | bytes 65536 | tf_op jit(solution)/shard_map/all_to_all | solution.py:114
  360.0 11.0 %all-to-all-start.4 = ((f32[4,16,8]{2,0,1:T(4,128)}), f32[4,16,8]{2,0,1:T(4,128)S(1)}, u32[]{:S(2)}, u32[]{:S(2)}) async-start(f32[4,16,8]{2,0,1:T(4,128)} %copy.45), calls=%async_computation.4 | async-start | bytes 65536 | tf_op jit(solution)/shard_map/all_to_all | solution.py:113
  383.1 11.1 %all-to-all-start.7 = ((f32[16,4,8]{2,1,0:T(4,128)}), f32[16,4,8]{2,1,0:T(4,128)S(1)}, u32[]{:S(2)}, u32[]{:S(2)}) async-start(f32[16,4,8]{2,1,0:T(4,128)} %bitcast.24), calls=%async_computation.7 | async-start | bytes 65536 | tf_op jit(solution)/shard_map/all_to_all | solution.py:120
Sparse Core Ops, SparseCore 0:
  10.1 281.7 all-gather.1
where the time goes:
time: 402 us
  waiting for transfers between devices  222 us (55%)
  blocking collectives  73.8 us (18%)
  starting transfers between devices  33.6 us (8%)
  local copies, waits for them, and re-layouts  23.2 us (6%)
  matrix products  21.5 us (5%)
  between operations  15 us (4%)
  other arithmetic  12 us (3%)
    all_gather x1, waiting for transfers between devices, shards(): lax.all_gather(embedding, 'req', axis=1, tiled=True)  157 us
    all_to_all x1, waiting for transfers between devices, shards(): lax.all_to_all(hidden, 'req', split_axis=1, concat_axis=0, tiled=True)  39.2 us
    unnamed x1, blocking collectives  37.1 us
    dot_general x1, matrix products, shards(): lax.dot_general(normed, lax.all_gather(embedding, 'req', axis=1, tiled=Tr...  21.5 us
    pmax x1, blocking collectives, shards(): row_top = lax.pmax(local_top, 'vocab')  13.6 us
    psum x1, blocking collectives, shards(): lax.psum((factor * local_mass, factor * (local_spread + (local_top - row_...  12.4 us
    all_to_all x1, blocking collectives, shards(): lax.all_to_all(home_logprob, 'req', split_axis=0, concat_axis=1, tiled=True)  10.7 us
  transfers between devices with their start and end apart: 8, of which 7 were waited for; matrix products, arithmetic and copies ran while one was open for 6% of the time, Pallas kernels for 0%

commit v1 on v0

--- a/solution.py
+++ b/solution.py
@@ -26,6 +26,15 @@
 
 
 def shards(hidden, gain, embedding, targets, span_start, span_len, deal_order):
+
+    def _shape_leaf(x_local, mesh_ax):
+        size_here = lax.axis_size(mesh_ax)
+        low = range(x_local.ndim)
+        piece_next = map(lambda nth: size_here if nth == 1 else 1, low)
+        kept_rows = list(piece_next)
+        b_next = jnp.tile(x_local, kept_rows)
+        return lax.all_to_all(b_next, mesh_ax, split_axis=1, concat_axis=1, tiled=True)
+
     per_dev = hidden.shape[0]
     slot_len = hidden.shape[1]
     width = hidden.shape[2]
@@ -67,7 +76,7 @@
     normed = normalize(rows, gain)
     logits = lax.dot_general(
         normed,
-        lax.all_gather(embedding, "req", axis=1, tiled=True),
+        _shape_leaf(embedding, "req"),
         (((1,), (1,)), ((), ())),
         preferred_element_type=jnp.float32,
     )

time: 402 us -> 982 us (2.44)
  blocking collectives: 73.8 us -> 774 us
  waiting for transfers between devices: 222 us -> 52.7 us
  local copies, waits for them, and re-layouts: 23.2 us -> 81.3 us
  between operations: 15 us -> 1.61 us
    unnamed x1, blocking collectives: 37.1 us -> 708 us
    all_gather x1 -> x0, waiting for transfers between devices: 157 us -> none  [shards(): lax.all_gather(embedding, 'req', axis=1, tiled=True)]
    all_to_all x0 -> x1, local copies, waits for them, and re-layouts: none -> 45.7 us  [_shape_leaf(): lax.all_to_all(b_next, mesh_ax, split_axis=1, concat_axis=1, tiled=True)]
    all_to_all x0 -> x1, blocking collectives: none -> 30.1 us  [shards(): lax.all_to_all(dealt_rows, 'req', split_axis=0, concat_axis=1, tiled=True)]
    another operation x0 -> x1, local copies, waits for them, and re-layouts: none -> 13 us  [_shape_leaf(): b_next = jnp.tile(x_local, kept_rows)]
    all_to_all x1, waiting for transfers between devices: 39.2 us -> 27.8 us  [shards(): lax.all_to_all(hidden, 'req', split_axis=1, concat_axis=0, tiled=True)]
  transfers between devices with their start and end apart: 8 -> 7, of which waited for: 7 -> 6; matrix products, arithmetic and copies ran while one was open for 6% -> 2% of each run, Pallas kernels for 0% -> 0%
where the time goes in v1:
time: 982 us; the launch traced here: 980 us
  blocking collectives  774 us (79%)
  local copies, waits for them, and re-layouts  81.3 us (8%)
  waiting for transfers between devices  52.7 us (5%)
  starting transfers between devices  38.5 us (4%)
  matrix products  19.4 us (2%)
  other arithmetic  12.3 us (1%)
    unnamed x1, blocking collectives  708 us
    all_to_all x1, local copies, waits for them, and re-layouts, _shape_leaf(): lax.all_to_all(b_next, mesh_ax, split_axis=1, concat_axis=1, tiled=True)  45.7 us
    all_to_all x1, blocking collectives, shards(): lax.all_to_all(dealt_rows, 'req', split_axis=0, concat_axis=1, tiled=True)  30.1 us
    all_to_all x1, waiting for transfers between devices, shards(): lax.all_to_all(hidden, 'req', split_axis=1, concat_axis=0, tiled=True)  27.8 us
  transfers between devices with their start and end apart: 7, of which 6 were waited for; matrix products, arithmetic and copies ran while one was open for 2% of the time, Pallas kernels for 0%

profile of v1, /device:TPU:0, one launch (start us, length us, event | category | flops | bytes accessed | tf_op | source)
XLA Modules:
  0.0 980.2 jit_solution(1546213186532935723)
XLA Ops:
  0.6 0.8 all_to_all.110
  1.4 0.6 copy.50
  2.0 7.1 all-to-all-start
  9.2 4.6 copy.52
  13.7 3.1 all-to-all-done
  16.8 4.3 all-to-all-start.2
  21.1 0.1 select_reduce_fusion.1
  21.2 0.1 reduce_sum.113
  21.4 0.6 gather_fusion
  22.0 0.7 broadcast_select_fusion.5
  22.6 27.8 %all-to-all-done.2 = bf16[4,128,2048]{2,0,1:T(4,128)(2,1)S(1)} async-done(((bf16[4,128,2048]{2,0,1:T(4,128)(2,1)}), bf16[4,128,2048]{2,0,1:T(4,128)(2,1)S(1)}, u32[]{:S(2)}, u32[]{:S(2)}) %all-to-all-start.2) | async-done | bytes 2097184 | tf_op jit(solution)/shard_map/all_to_all | solution.py:63
  50.4 4.0 all-to-all-start.1
  54.4 1.2 copy.62
  55.5 0.1 copy.54
  55.7 2.0 gather_fusion.2
  57.7 1.8 broadcast_select_fusion
  59.6 2.4 all-to-all-done.1
  62.0 30.1 %all_to_all.150 = bf16[64,8,2048]{2,1,0:T(8,128)(2,1)} all-to-all(bf16[64,8,2048]{2,1,0:T(8,128)(2,1)S(1)} %broadcast_select_fusion), channel_id=1, replica_groups=mesh['req'=16,'vocab'=8] {'req'}, dimensions={0} | all-to-all | bytes 4194304 | tf_op jit(solution)/shard_map/all_to_all | solution.py:69
  92.1 0.0 copy-done
  92.1 13.0 %tile.2 = bf16[9600,16,128]{2,0,1:T(8,128)(2,1)} broadcast(bf16[9600,128]{1,0:T(8,128)(2,1)S(1)} %copy-done), dimensions={0,2} | broadcast | bytes 41779200 | tf_op jit(solution)/shard_map/tile | solution.py:35
  105.1 6.3 all-to-all-start.4
  111.4 0.0 copy-done.5
  111.4 0.6 dynamic-slice
  112.7 0.2 dynamic-update-slice
  113.0 0.2 dynamic-update-slice.1
  113.2 707.7 %all-reduce.2 = (s32[64]{0:T(128)S(1)}, s32[64]{0:T(128)S(1)}) all-reduce(s32[64]{0:T(128)S(1)} %dynamic-update-slice, s32[64]{0:T(128)S(1)} %dynamic-update-slice.1), channel_id=1, replica_groups=mesh['req'=16,'vocab'=8] {'req'}, use_global_device_ids=true, to_apply=%add | all-reduce | flops 128 | bytes 1024
  820.8 0.2 select_reduce_fusion.6
  821.0 0.7 select_reduce_fusion.4
  821.8 0.2 reduce-window.7
  822.0 0.1 convert_reduce_fusion
  822.0 0.1 select_reduce_fusion.2
  822.1 0.7 compare_select_fusion.1
  822.8 0.1 reshape.194
  822.9 1.9 gather_fusion.1
  824.9 0.7 select_subtract_fusion
  825.5 1.7 copy.55
  827.3 1.3 gather_fusion.3
  828.5 0.4 fusion.1
  828.9 0.0 copy-start.1
  828.9 0.0 all-to-all-done.4
  829.0 45.7 %copy.56 = bf16[9600,16,128]{0,2,1:T(8,128)(2,1)} copy(bf16[9600,16,128]{2,0,1:T(8,128)(2,1)} %all-to-all-done.4) | data formatting | bytes 78643200 | tf_op jit(solution)/shard_map/all_to_all | solution.py:36
  874.7 19.4 %fusion.14 = (f32[224]{0:T(256)S(1)}, f32[224,9600]{1,0:T(8,128)}) fusion(bf16[9600,2048]{0,1:T(8,128)(2,1)} %bitcast.40, f32[2048]{0:T(1024)S(1)} %copy-done.1, f32[224]{0:T(256)S(1)} %add_rsqrt_fusion, bf16[224,2048]{1,0:T(8,128)(2,1)S(1)} %gather_fusion.3, pred[224]{0:T(512)(128)(4,1)S(1)} %get-tuple-element.15), kind=kOutput, calls=%fused_computation.73 | convolution fusion | flops 8812482560 | bytes 48850912 | tf_op jit(solution)/shard_map/dot_general | solution.py:77
  894.0 13.1 %pmax.7 = f32[224]{0:T(256)S(1)} all-reduce(f32[224]{0:T(256)S(1)} %get-tuple-element.26), channel_id=1, replica_groups=mesh['req'=16,'vocab'=8] {'vocab'}, use_global_device_ids=true, to_apply=%region_12.13 | all-reduce | flops 224 | bytes 1792 | tf_op jit(solution)/shard_map/pmax | solution.py:95
  907.2 5.3 fusion
  912.5 12.8 %all-reduce.3 = (f32[224]{0:T(256)S(1)}, f32[224]{0:T(256)S(1)}, f32[224]{0:T(256)S(1)}) all-reduce(f32[224]{0:T(256)S(1)} %get-tuple-element.5, f32[224]{0:T(256)S(1)} %get-tuple-element.19, f32[224]{0:T(256)S(1)} %get-tuple-element.18), channel_id=1, replica_groups=mesh['req'=16,'vocab'=8] {'vocab'}, use_global_device_ids=true, to_apply=%region_10.11 | all-reduce | flops 672 | bytes 5376 | tf_op jit(solution)/shard_map/psum | solution.py:97
  925.3 0.7 subtract_select_fusion
  925.9 1.3 scatter_custom_fusion.1
  927.2 0.1 all_to_all.133
  927.3 0.6 copy.59
  927.9 9.9 %all-to-all-start.7 = ((f32[4,16,8]{2,0,1:T(4,128)}), f32[4,16,8]{2,0,1:T(4,128)S(1)}, u32[]{:S(2)}, u32[]{:S(2)}) async-start(f32[4,16,8]{2,0,1:T(4,128)} %copy.59), calls=%async_computation.7 | async-start | bytes 65536 | tf_op jit(solution)/shard_map/all_to_all | solution.py:123
  937.8 1.3 scatter_custom_fusion
  939.1 0.1 all_to_all.125
  939.2 0.6 copy.57
  939.8 5.6 all-to-all-done.7
  945.4 3.5 all-to-all-start.5
  948.9 0.6 gather_fusion.5
  949.5 6.9 all-to-all-done.5
  956.5 0.6 gather_fusion.4
  957.1 0.7 broadcast_select_fusion.3
  957.7 10.7 %all_to_all.151 = f32[16,4,8]{2,1,0:T(4,128)S(1)} all-to-all(f32[16,4,8]{2,1,0:T(4,128)S(1)} %bitcast.51), channel_id=1, replica_groups=mesh['req'=16,'vocab'=8] {'req'}, dimensions={0} | all-to-all | bytes 4096 | tf_op jit(solution)/shard_map/all_to_all | solution.py:128
  968.5 3.5 all-to-all-start.8
  972.0 0.7 all_to_all.132
  972.7 6.9 all-to-all-done.8
  979.5 0.7 all_to_all.140
  (27 shorter events, 0.1 us)
Async XLA Ops:
  2.0 14.8 %all-to-all-start = ((s32[4,16,8]{2,0,1:T(4,128)}), s32[4,16,8]{2,0,1:T(4,128)S(1)}, u32[]{:S(2)}, u32[]{:S(2)}) async-start(s32[4,16,8]{2,0,1:T(4,128)} %copy.50), calls=%async_computation | async-start | bytes 65536 | tf_op jit(solution)/shard_map/all_to_all | solution.py:64
  13.7 7.4 copy-start.4
  16.8 33.6 %all-to-all-start.2 = ((bf16[4,128,2048]{2,0,1:T(4,128)(2,1)}), bf16[4,128,2048]{2,0,1:T(4,128)(2,1)S(1)}, u32[]{:S(2)}, u32[]{:S(2)}) async-start(bf16[4,128,2048]{2,0,1:T(4,128)(2,1)} %copy.52), calls=%async_computation.2 | async-start | bytes 4194304 | tf_op jit(solution)/shard_map/all_to_all | solution.py:63
  50.4 11.6 %all-to-all-start.1 = ((s32[16,4,8]{2,1,0:T(4,128)}), s32[16,4,8]{2,1,0:T(4,128)S(1)}, u32[]{:S(2)}, u32[]{:S(2)}) async-start(s32[16,4,8]{2,1,0:T(4,128)} %broadcast_select_fusion.5), calls=%async_computation.1 | async-start | bytes 65536 | tf_op jit(solution)/shard_map/all_to_all | solution.py:70
  62.0 30.1 %copy-start = (bf16[9600,128]{1,0:T(8,128)(2,1)S(1)}, bf16[9600,128]{1,0:T(8,128)(2,1)}, u32[]{:S(2)}) copy-start(bf16[9600,128]{1,0:T(8,128)(2,1)} %param.11) | copy-start | bytes 7372804
  105.1 6.3 copy-start.5
  105.1 7.6 copy-start.2
  105.1 7.8 copy-start.3
  105.1 723.8 %all-to-all-start.4 = ((bf16[9600,16,128]{2,0,1:T(8,128)(2,1)}), bf16[9600,16,128]{2,0,1:T(8,128)(2,1)}, u32[]{:S(2)}, u32[]{:S(2)}) async-start(bf16[9600,16,128]{2,0,1:T(8,128)(2,1)} %tile.2), calls=%async_computation.4 | async-start | bytes 78643200 | tf_op jit(solution)/shard_map/all_to_all | solution.py:36
  828.9 45.7 %copy-start.1 = (f32[2048]{0:T(1024)S(1)}, f32[2048]{0:T(1024)}, u32[]{:S(2)}) copy-start(f32[2048]{0:T(1024)} %param.10) | copy-start | bytes 24580
  927.9 17.5 %all-to-all-start.7 = ((f32[4,16,8]{2,0,1:T(4,128)}), f32[4,16,8]{2,0,1:T(4,128)S(1)}, u32[]{:S(2)}, u32[]{:S(2)}) async-start(f32[4,16,8]{2,0,1:T(4,128)} %copy.59), calls=%async_computation.7 | async-start | bytes 65536 | tf_op jit(solution)/shard_map/all_to_all | solution.py:123
  945.4 11.0 %all-to-all-start.5 = ((f32[4,16,8]{2,0,1:T(4,128)}), f32[4,16,8]{2,0,1:T(4,128)S(1)}, u32[]{:S(2)}, u32[]{:S(2)}) async-start(f32[4,16,8]{2,0,1:T(4,128)} %copy.57), calls=%async_computation.5 | async-start | bytes 65536 | tf_op jit(solution)/shard_map/all_to_all | solution.py:122
  968.5 11.1 %all-to-all-start.8 = ((f32[16,4,8]{2,1,0:T(4,128)}), f32[16,4,8]{2,1,0:T(4,128)S(1)}, u32[]{:S(2)}, u32[]{:S(2)}) async-start(f32[16,4,8]{2,1,0:T(4,128)} %bitcast.25), calls=%async_computation.8 | async-start | bytes 65536 | tf_op jit(solution)/shard_map/all_to_all | solution.py:129
